TPU v7x, 32 devices: a whole 2x2x4 slice. The times are simulated.
32 devices in a mesh: group: 4 (over y, core), tile: 8 (over z, x).
Axes of the slice: x: 2, y: 2, z: 4, core: 2. Of those that a mesh axis runs over, the one named last changes fastest.
Arguments:
- maps: bfloat16 [32, 256, 128, 128], P('group', 'tile'), may hold values from -6 to 6
- first_weight: bfloat16 [3, 3, 128, 256], replicated, may hold values from -0.1875 to 0.1875
- second_weight: bfloat16 [3, 3, 256, 256], replicated, may hold values from -0.125 to 0.125
- out_grad: bfloat16 [32, 128, 64, 256], P(('group', 'tile')), may hold values from -0.0234375 to 0.0234375
Outputs:
- conv_out: bfloat16 [32, 128, 64, 256], P(('group', 'tile'))
- weight_grad: float32 [256, 3, 3, 256], P(('group', 'tile'))
All inputs are finite; a program needn't handle non-finite values.
Results may differ from a plain program's by a relative error of at most 0.0051.
Values may be sent and summed in bfloat16 or wider, within the bound.
No kernel may reach another device: no remote copies, remote signals or barrier semaphores. Data moves between devices by JAX's collectives and lax.ppermute only.
A program may use at most 192 MiB of HBM per device.

v0:
```python
import jax
import jax.numpy as jnp
from jax import lax
from jax.sharding import PartitionSpec as P


def shifted_2(shard, axis, by):
    length = lax.axis_size(axis)
    pairs = [(i, i + by) for i in range(length) if 0 <= i + by < length]
    return lax.ppermute(shard, axis, pairs)


def shift_cols_right(slab):
    zero_col = jnp.zeros_like(slab[:, :, :1])
    return jnp.concatenate([zero_col, slab[:, :, :-1]], axis=2)


def shift_cols_left(slab):
    zero_col = jnp.zeros_like(slab[:, :, :1])
    return jnp.concatenate([slab[:, :, 1:], zero_col], axis=2)


def first_conv(source, upper_row, first_weight):
    images, rows, width, inputs = source.shape
    outputs = first_weight.shape[3]
    paired = source.reshape(images, rows // 2, 2, width // 2, 2 * inputs)
    even_rows = paired[:, :, 0]
    odd_rows = paired[:, :, 1]
    upper_paired = upper_row.reshape(images, 1, width // 2, 2 * inputs)
    odd_above = jnp.concatenate([upper_paired, odd_rows[:, :-1]], axis=1)
    sources = [odd_above, even_rows, odd_rows]
    total = jnp.zeros((images, rows // 2, width // 2, outputs), jnp.float32)
    for tap_row in range(3):
        wide_kernel = first_weight[tap_row, 1:3].reshape(2 * inputs, outputs)
        total = total + jnp.dot(sources[tap_row], wide_kernel, preferred_element_type=jnp.float32)
    halves = jnp.concatenate([piece[..., inputs:] for piece in sources], axis=-1)
    narrow_kernel = first_weight[:, 0].reshape(3 * inputs, outputs)
    total = total + jnp.dot(
        shift_cols_right(halves), narrow_kernel, preferred_element_type=jnp.float32
    )
    return jnp.maximum(total, 0.0).astype(jnp.bfloat16)


def local(maps, first_weight, second_weight, out_grad):
    tiles = lax.axis_size("tile")
    images, height, width, inputs = maps.shape
    outputs = first_weight.shape[3]
    owned = images // tiles
    upper_row = shifted_2(maps[:, height - 1 : height], "tile", 1)
    local_hidden = first_conv(maps, upper_row, first_weight)
    half_rows = height // 2
    arrived = lax.all_to_all(
        local_hidden.reshape(tiles, owned, half_rows, width // 2, outputs),
        "tile",
        split_axis=0,
        concat_axis=2,
        tiled=True,
    )
    hidden = arrived.reshape(owned, half_rows * tiles, width // 2, outputs)
    out_rows = hidden.shape[1]
    out_cols = hidden.shape[2]
    row_padded = jnp.pad(hidden, ((0, 0), (1, 1), (0, 0), (0, 0)))
    shifted = [shift_cols_right(row_padded), row_padded, shift_cols_left(row_padded)]
    total = jnp.zeros((owned, out_rows, out_cols, outputs), jnp.float32)
    for tap_row in range(3):
        for tap_col in range(3):
            window = shifted[tap_col][:, tap_row : tap_row + out_rows]
            total = total + jnp.dot(
                window, second_weight[tap_row, tap_col], preferred_element_type=jnp.float32
            )
    conv_out = total.astype(jnp.bfloat16)
    devices = lax.axis_size("group") * tiles
    selected = out_grad.reshape(-1, lax.axis_size(("group", "tile")) * (outputs // devices))
    terms = []
    for tap_row in range(3):
        for tap_col in range(3):
            window = shifted[tap_col][:, tap_row : tap_row + out_rows].reshape(-1, outputs)
            terms.append(
                lax.dot_general(
                    selected, window, (((0,), (0,)), ((), ())), preferred_element_type=jnp.float32
                )
            )
    summed = lax.psum_scatter(
        jnp.stack(terms, axis=1).reshape(
            lax.axis_size(("group", "tile")) * (outputs // devices), 9 * outputs
        ),
        ("group", "tile"),
        scatter_dimension=0,
        tiled=True,
    )
    weight_grad = summed.reshape(-1, 3, 3, outputs)
    return (conv_out, weight_grad)


def solution(mesh):
    return jax.shard_map(
        local,
        mesh=mesh,
        in_specs=(P("group", "tile", None, None), P(), P(), P(("group", "tile"), None, None, None)),
        out_specs=(P(("group", "tile"), None, None, None), P(("group", "tile"), None, None, None)),
        check_vma=False,
    )
```

profile of v0, /device:TPU:0, one launch (start us, length us, event | category | flops | bytes accessed | tf_op | source)
XLA Modules:
  0.0 348.4 jit_solution(9022107546819320369)
XLA Ops:
  8.2 5.0 %collective-permute-start = (bf16[8,1,128,128]{3,2,1,0:T(8,128)(2,1)S(1)}, bf16[8,1,128,128]{3,2,1,0:T(8,128)(2,1)S(1)}, u32[]{:S(2)}, u32[]{:S(2)}) collective-permute-start(bf16[8,1,128,128]{3,2,1,0:T(8,128)(2,1)S(1)} %slice.103), channel_id=1, source_target_pairs={{0,1},{1,2},{2,3},{3,4},{4,5},{5,6},{6,7},{8,9},{9,10},{10,11},{11... | collective-permute-start | bytes 786440 | tf_op jit(solution)/shard_map/ppermute | solution.py:10
  13.2 12.9 %reshape.106 = bf16[8,16,2,64,256]{4,3,2,1,0:T(8,128)(2,1)} reshape(bf16[8,32,128,128]{3,2,1,0:T(8,128)(2,1)} %param.4) | data formatting | bytes 16777216 | tf_op jit(solution)/shard_map/reshape | solution.py:26
  26.2 6.8 %fusion.185 = f32[8,16,64,256]{3,2,1,0:T(8,128)} fusion(bf16[256,256,1,1]{1,0,3,2:T(8,128)(2,1)S(1)} %bitcast.263, bf16[8,16,2,64,256]{4,3,2,1,0:T(8,128)(2,1)} %reshape.106), kind=kOutput, calls=%fused_computation.155 | convolution fusion | flops 1073741824 | bytes 12713984 | tf_op jit(solution)/shard_map/dot_general | solution.py:35
  33.0 4.5 %fusion.186 = f32[8,16,64,256]{3,2,1,0:T(8,128)} fusion(bf16[256,256,1,1]{1,0,3,2:T(8,128)(2,1)S(1)} %bitcast.262, bf16[8,16,2,64,256]{4,3,2,1,0:T(8,128)(2,1)S(1)} %bitcast.242), kind=kOutput, calls=%fused_computation.156 | convolution fusion | flops 1073741824 | bytes 12713984 | tf_op jit(solution)/shard_map/dot_general | solution.py:35
  38.7 2.4 slice.135
  41.1 1.8 slice.138
  42.9 1.8 slice.137
  44.8 3.5 %fusion.19 = f32[8,16,64,256]{3,2,1,0:T(8,128)S(1)} fusion(bf16[256,256,1,1]{1,0,3,2:T(8,128)(2,1)S(1)} %bitcast.261, bf16[8,15,64,256]{3,2,1,0:T(8,128)(2,1)} %slice.135, bf16[8,1,64,256]{3,2,1,0:T(8,128)(2,1)S(1)} %reshape.105), kind=kOutput, calls=%fused_computation.20 | convolution fusion | flops 1075838976 | bytes 12713984 | tf_op jit(solution)/shard_map/dot_general | solution.py:35
  48.3 10.3 %fusion.17 = bf16[8,1,16,64,256]{4,3,2,1,0:T(8,128)(2,1)} fusion(f32[8,16,64,256]{3,2,1,0:T(8,128)} %fusion.185, f32[8,16,64,256]{3,2,1,0:T(8,128)S(1)} %fusion.19, f32[8,16,64,256]{3,2,1,0:T(8,128)} %fusion.186, bf16[384,256,1,1]{1,0,3,2:T(8,128)(2,1)S(1)} %bitcast.260, bf16[8,16,64,128]{3,2,1,0:T(8,128)(2,1)} %slice.138, ...), kind=kOutput, calls=%fused_computation.16 | convolution fusion | flops 1661992960 | bytes 37945344 | tf_op jit(solution)/shard_map/dot_general | solution.py:38
  58.6 98.4 %all_to_all.4 = bf16[8,1,16,64,256]{4,3,2,1,0:T(8,128)(2,1)S(1)} all-to-all(bf16[8,1,16,64,256]{4,3,2,1,0:T(8,128)(2,1)} %fusion.17), channel_id=1, replica_groups=mesh['group'=4,'tile'=8] {'tile'}, dimensions={0} | all-to-all | bytes 8388608 | tf_op jit(solution)/shard_map/all_to_all | solution.py:52
  157.1 2.4 copy.51
  159.5 4.8 %pad_slice_fusion.1 = (bf16[1,130,63,256]{3,1,2,0:T(8,128)(2,1)S(1)}, bf16[1,130,63,256]{3,1,2,0:T(8,128)(2,1)S(1)}) fusion(bf16[1,128,64,256]{3,1,2,0:T(8,128)(2,1)S(1)} %bitcast.243), kind=kLoop, calls=%fused_computation.78 | loop fusion | bytes 12580864 | tf_op jit(solution)/shard_map/slice | solution.py:15
  164.4 4.5 %fusion.25 = f32[128,64,256]{2,0,1:T(8,128)} fusion(bf16[1,130,63,256]{3,1,2,0:T(8,128)(2,1)S(1)} %get-tuple-element.11, bf16[3,3,256,256]{3,2,1,0:T(8,128)(2,1)S(1)} %copy-done.3), kind=kOutput, calls=%fused_computation.26 | convolution fusion | flops 1073741824 | bytes 12906496 | tf_op jit(solution)/shard_map/dot_general | solution.py:68
  168.9 4.5 %fusion.37 = f32[128,64,256]{2,0,1:T(8,128)} fusion(bf16[1,130,63,256]{3,1,2,0:T(8,128)(2,1)S(1)} %get-tuple-element.11, bf16[3,3,256,256]{3,2,1,0:T(8,128)(2,1)S(1)} %copy-done.3), kind=kOutput, calls=%fused_computation.38 | convolution fusion | flops 1073741824 | bytes 12906496 | tf_op jit(solution)/shard_map/dot_general | solution.py:68
  173.4 4.5 %fusion.33 = f32[128,64,256]{2,0,1:T(8,128)} fusion(bf16[1,130,63,256]{3,1,2,0:T(8,128)(2,1)S(1)} %get-tuple-element.10, bf16[3,3,256,256]{3,2,1,0:T(8,128)(2,1)S(1)} %copy-done.3), kind=kOutput, calls=%fused_computation.34 | convolution fusion | flops 1073741824 | bytes 12906496 | tf_op jit(solution)/shard_map/dot_general | solution.py:68
  177.8 4.5 %fusion.41 = f32[128,64,256]{2,0,1:T(8,128)} fusion(bf16[1,130,63,256]{3,1,2,0:T(8,128)(2,1)S(1)} %get-tuple-element.10, bf16[3,3,256,256]{3,2,1,0:T(8,128)(2,1)S(1)} %copy-done.3), kind=kOutput, calls=%fused_computation.42 | convolution fusion | flops 1073741824 | bytes 12906496 | tf_op jit(solution)/shard_map/dot_general | solution.py:68
  182.3 4.5 %fusion.45 = f32[128,64,256]{2,0,1:T(8,128)} fusion(bf16[1,130,63,256]{3,1,2,0:T(8,128)(2,1)S(1)} %get-tuple-element.11, bf16[3,3,256,256]{3,2,1,0:T(8,128)(2,1)S(1)} %copy-done.3), kind=kOutput, calls=%fused_computation.46 | convolution fusion | flops 1073741824 | bytes 12906496 | tf_op jit(solution)/shard_map/dot_general | solution.py:68
  186.8 4.5 %fusion.53 = f32[128,64,256]{2,0,1:T(8,128)} fusion(bf16[1,130,63,256]{3,1,2,0:T(8,128)(2,1)S(1)} %get-tuple-element.10, bf16[3,3,256,256]{3,2,1,0:T(8,128)(2,1)S(1)} %copy-done.3), kind=kOutput, calls=%fused_computation.54 | convolution fusion | flops 1073741824 | bytes 12906496 | tf_op jit(solution)/shard_map/dot_general | solution.py:68
  191.3 4.5 %fusion.29 = f32[128,64,256]{2,0,1:T(8,128)} fusion(bf16[1,128,64,256]{3,1,2,0:T(8,128)(2,1)S(1)} %bitcast.244, bf16[3,3,256,256]{3,2,1,0:T(8,128)(2,1)S(1)} %copy-done.3), kind=kOutput, calls=%fused_computation.30 | convolution fusion | flops 1073741824 | bytes 12713984 | tf_op jit(solution)/shard_map/dot_general | solution.py:68
  195.8 5.1 %fusion.93 = f32[256,9,256]{0,2,1:T(8,128)S(1)} fusion(bf16[1,130,63,256]{3,1,2,0:T(8,128)(2,1)S(1)} %get-tuple-element.10, bf16[128,64,256]{2,1,0:T(8,128)(2,1)S(1)} %bitcast.250), kind=kOutput, calls=%fused_computation.92 | convolution fusion | flops 1073741824 | bytes 8649728 | tf_op jit(solution)/shard_map/dot_general | solution.py:79
  200.9 5.6 %fusion.99 = f32[256,9,256]{0,2,1:T(8,128)S(1)} fusion(f32[256,9,256]{0,2,1:T(8,128)S(1)} %fusion.93, bf16[1,128,64,256]{3,1,2,0:T(8,128)(2,1)S(1)} %bitcast.245, bf16[128,64,256]{2,1,0:T(8,128)(2,1)S(1)} %bitcast.251), kind=kOutput, calls=%fused_computation.94 | convolution fusion | flops 1073741824 | bytes 8650752 | tf_op jit(solution)/shard_map/dot_general | solution.py:79
  206.5 5.3 %fusion.105 = f32[256,9,256]{0,2,1:T(8,128)S(1)} fusion(f32[256,9,256]{0,2,1:T(8,128)S(1)} %fusion.99, bf16[1,130,63,256]{3,1,2,0:T(8,128)(2,1)S(1)} %get-tuple-element.11, bf16[128,64,256]{2,1,0:T(8,128)(2,1)S(1)} %bitcast.252), kind=kOutput, calls=%fused_computation.96 | convolution fusion | flops 1073741824 | bytes 8843264 | tf_op jit(solution)/shard_map/dot_general | solution.py:79
  211.8 5.5 %fusion.111 = f32[256,9,256]{0,2,1:T(8,128)S(1)} fusion(f32[256,9,256]{0,2,1:T(8,128)S(1)} %fusion.105, bf16[1,130,63,256]{3,1,2,0:T(8,128)(2,1)S(1)} %get-tuple-element.10, bf16[128,64,256]{2,1,0:T(8,128)(2,1)S(1)} %bitcast.253), kind=kOutput, calls=%fused_computation.98 | convolution fusion | flops 1073741824 | bytes 8843264 | tf_op jit(solution)/shard_map/dot_general | solution.py:79
  218.7 5.6 %fusion.117 = f32[256,9,256]{0,2,1:T(8,128)S(1)} fusion(f32[256,9,256]{0,2,1:T(8,128)S(1)} %fusion.138, bf16[1,130,63,256]{3,1,2,0:T(8,128)(2,1)S(1)} %get-tuple-element.11, bf16[128,64,256]{2,1,0:T(8,128)(2,1)S(1)} %bitcast.255), kind=kOutput, calls=%fused_computation.100 | convolution fusion | flops 1073741824 | bytes 8843264 | tf_op jit(solution)/shard_map/dot_general | solution.py:79
  224.3 5.7 %fusion.123 = f32[256,9,256]{0,2,1:T(8,128)S(1)} fusion(f32[256,9,256]{0,2,1:T(8,128)S(1)} %fusion.117, bf16[1,130,63,256]{3,1,2,0:T(8,128)(2,1)S(1)} %get-tuple-element.10, bf16[128,64,256]{2,1,0:T(8,128)(2,1)S(1)} %bitcast.256), kind=kOutput, calls=%fused_computation.102 | convolution fusion | flops 1073741824 | bytes 8843264 | tf_op jit(solution)/shard_map/dot_general | solution.py:79
  230.0 5.6 %fusion.129 = f32[256,9,256]{0,2,1:T(8,128)S(1)} fusion(f32[256,9,256]{0,2,1:T(8,128)S(1)} %fusion.123, bf16[1,128,64,256]{3,1,2,0:T(8,128)(2,1)S(1)} %bitcast.246, bf16[128,64,256]{2,1,0:T(8,128)(2,1)S(1)} %bitcast.257), kind=kOutput, calls=%fused_computation.104 | convolution fusion | flops 1073741824 | bytes 8650752 | tf_op jit(solution)/shard_map/dot_general | solution.py:79
  235.6 5.7 %fusion.135 = f32[256,9,256]{0,2,1:T(8,128)S(1)} fusion(f32[256,9,256]{0,2,1:T(8,128)S(1)} %fusion.129, bf16[1,130,63,256]{3,1,2,0:T(8,128)(2,1)S(1)} %get-tuple-element.11, bf16[128,64,256]{2,1,0:T(8,128)(2,1)S(1)} %bitcast.258), kind=kOutput, calls=%fused_computation.106 | convolution fusion | flops 1073741824 | bytes 8843264 | tf_op jit(solution)/shard_map/dot_general | solution.py:79
  241.4 2.0 copy.69
  243.4 6.7 %fusion.49 = f32[128,64,256]{2,0,1:T(8,128)} fusion(bf16[1,128,64,256]{3,1,2,0:T(8,128)(2,1)} %bitcast.247, bf16[3,3,256,256]{3,2,1,0:T(8,128)(2,1)S(1)} %copy-done.3), kind=kOutput, calls=%fused_computation.50 | convolution fusion | flops 1073741824 | bytes 12713984 | tf_op jit(solution)/shard_map/dot_general | solution.py:68
  250.1 25.8 %fusion.18 = bf16[1,128,64,256]{3,1,2,0:T(8,128)(2,1)} fusion(f32[128,64,256]{2,0,1:T(8,128)} %fusion.25, f32[128,64,256]{2,0,1:T(8,128)} %fusion.29, f32[128,64,256]{2,0,1:T(8,128)} %fusion.33, f32[128,64,256]{2,0,1:T(8,128)} %fusion.37, f32[128,64,256]{2,0,1:T(8,128)} %fusion.41, f32[128,64,256]{2,0,1:T(8,128)} %fusion.45, f32[128,64,256]{2,0,1:T(8,128)} %fusion.53, ...), kind=kOutput, calls=%fused_computation.17 | convolution fusion | flops 1092616192 | bytes 75628544 | tf_op jit(solution)/shard_map/dot_general | solution.py:68
  275.9 6.6 %copy.70 = bf16[1,128,64,256]{3,2,1,0:T(8,128)(2,1)} copy(bf16[1,128,64,256]{3,1,2,0:T(8,128)(2,1)} %fusion.18) | data formatting | bytes 8388608
  282.5 58.8 %reduce-scatter.2.cloned.1.call-done = f32[8,2304]{1,0:T(8,128)} async-done(((f32[256,2304]{1,0:T(8,128)}), f32[8,2304]{1,0:T(8,128)}) %reduce-scatter.2.cloned.1.call-update) | async-done | bytes 73744 | tf_op jit(solution)/shard_map/reduce_scatter | solution.py:83
  (25 shorter events, 3.7 us)
Async XLA Ops:
  7.2 334.2 %reduce-scatter.2.cloned.1.call-start = ((), (), s32[]{:S(2)}) async-start(), calls=%async_computation.2 | async-start | bytes 2433024 | tf_op jit(solution)/shard_map/reduce_scatter | solution.py:83
  8.2 17.9 %copy-start.4 = (bf16[3,3,128,256]{3,2,1,0:T(8,128)(2,1)S(1)}, bf16[3,3,128,256]{3,2,1,0:T(8,128)(2,1)}, u32[]{:S(2)}) copy-start(bf16[3,3,128,256]{3,2,1,0:T(8,128)(2,1)} %param.5) | copy-start | bytes 1769476
  8.2 36.5 %collective-permute-start = (bf16[8,1,128,128]{3,2,1,0:T(8,128)(2,1)S(1)}, bf16[8,1,128,128]{3,2,1,0:T(8,128)(2,1)S(1)}, u32[]{:S(2)}, u32[]{:S(2)}) collective-permute-start(bf16[8,1,128,128]{3,2,1,0:T(8,128)(2,1)S(1)} %slice.103), channel_id=1, source_target_pairs={{0,1},{1,2},{2,3},{3,4},{4,5},{5,6},{6,7},{8,9},{9,10},{10,11},{11... | collective-permute-start | bytes 786440 | tf_op jit(solution)/shard_map/ppermute | solution.py:10
  26.2 6.9 %slice-start = ((s8[8388608]{0:T(1024)(128)(4,1)}), s8[4194304]{0:T(1024)(128)(4,1)S(1)}, s32[]{:S(2)}) async-start(s8[8388608]{0:T(1024)(128)(4,1)} %bitcast.241), calls=%async_computation.3 | async-start | bytes 8388608
  26.2 6.8 %slice-start.1 = ((s8[8388608]{0:T(1024)(128)(4,1)}), s8[4194304]{0:T(1024)(128)(4,1)S(1)}, s32[]{:S(2)}) async-start(s8[8388608]{0:T(1024)(128)(4,1)} %bitcast.241), calls=%async_computation.4 | async-start | bytes 8388608
  44.8 3.5 %copy-start.1 = (bf16[8,15,64,256]{3,2,1,0:T(8,128)(2,1)S(1)}, bf16[8,15,64,256]{3,2,1,0:T(8,128)(2,1)}, u32[]{:S(2)}) copy-start(bf16[8,15,64,256]{3,2,1,0:T(8,128)(2,1)} %slice.135) | copy-start | bytes 11796484
  44.8 3.5 %slice-start.2 = ((bf16[3,3,128,256]{3,2,1,0:T(8,128)(2,1)}), bf16[3,1,128,256]{3,2,1,0:T(8,128)(2,1)S(1)}, s32[]{:S(2)}) async-start(bf16[3,3,128,256]{3,2,1,0:T(8,128)(2,1)} %param.5), calls=%async_computation.5 | async-start | bytes 393216 | tf_op jit(solution)/shard_map/slice | solution.py:37
  159.5 70.5 %copy-start = (bf16[8,1,16,64,256]{4,2,0,3,1:T(8,128)(2,1)}, bf16[8,1,16,64,256]{4,2,0,3,1:T(8,128)(2,1)S(1)}, u32[]{:S(2)}) copy-start(bf16[8,1,16,64,256]{4,2,0,3,1:T(8,128)(2,1)S(1)} %copy.51) | copy-start | bytes 12582916
  159.5 4.8 %copy-start.3 = (bf16[3,3,256,256]{3,2,1,0:T(8,128)(2,1)S(1)}, bf16[3,3,256,256]{3,2,1,0:T(8,128)(2,1)}, u32[]{:S(2)}) copy-start(bf16[3,3,256,256]{3,2,1,0:T(8,128)(2,1)} %param.6) | copy-start | bytes 3538948
  191.3 4.5 %copy-start.2 = (bf16[1,128,64,256]{3,2,1,0:T(8,128)(2,1)S(1)}, bf16[1,128,64,256]{3,2,1,0:T(8,128)(2,1)}, u32[]{:S(2)}) copy-start(bf16[1,128,64,256]{3,2,1,0:T(8,128)(2,1)} %param.7) | copy-start | bytes 12582916
Sparse Core Ops, SparseCore 0:
  243.5 97.8 reduce-scatter.1
where the time goes:
time: 355 us; the launch traced here: 348 us
  matrix products  135 us (38%)
  blocking collectives  98.4 us (28%)
  waiting for transfers between devices  58.8 us (17%)
  local copies, waits for them, and re-layouts  37 us (10%)
  between operations  14.4 us (4%)
  starting transfers between devices  5.03 us (1%)
    all_to_all x1, blocking collectives, local(): lax.all_to_all(local_hidden.reshape(tiles, owned, half_rows, width // 2,...  98.4 us
    dot_general x9, matrix products, local(): jnp.dot(window, second_weight[tap_row, tap_col], preferred_element_type=j...  63.9 us
    reduce_scatter x1, waiting for transfers between devices, local(): lax.psum_scatter(jnp.stack(terms, axis=1).reshape(lax.axis_size(('group',...  58.8 us
    dot_general x9, matrix products, local(): lax.dot_general(selected, window, (((0,), (0,)), ((), ())), preferred_ele...  45.5 us
    dot_general x3, matrix products, first_conv(): jnp.dot(sources[tap_row], wide_kernel, preferred_element_type=jnp.float32)  14.8 us
    reshape x1, local copies, waits for them, and re-layouts, first_conv(): paired = source.reshape(images, rows // 2, 2, width // 2, 2 * inputs)  12.9 us
    dot_general x1, matrix products, first_conv(): jnp.dot(shift_cols_right(halves), narrow_kernel, preferred_element_type=j...  10.3 us
  transfers between devices with their start and end apart: 2, of which 1 were waited for; matrix products, arithmetic and copies ran while one was open for 20% of the time, Pallas kernels for 0%

commit v1 on v0

--- a/solution.py
+++ b/solution.py
@@ -49,12 +49,20 @@
     upper_row = shifted_2(maps[:, height - 1 : height], "tile", 1)
     local_hidden = first_conv(maps, upper_row, first_weight)
     half_rows = height // 2
-    arrived = lax.all_to_all(
-        local_hidden.reshape(tiles, owned, half_rows, width // 2, outputs),
-        "tile",
-        split_axis=0,
-        concat_axis=2,
-        tiled=True,
+    arrived = jnp.concatenate(
+        lax.all_to_all(
+            jnp.stack(
+                jnp.split(
+                    local_hidden.reshape(tiles, owned, half_rows, width // 2, outputs),
+                    lax.axis_size("tile"),
+                    axis=0,
+                )
+            ),
+            "tile",
+            0,
+            0,
+        ),
+        axis=2,
     )
     hidden = arrived.reshape(owned, half_rows * tiles, width // 2, outputs)
     out_rows = hidden.shape[1]

time: 355 us -> 375 us (1.056)
  blocking collectives: 98.4 us -> 109 us
  local copies, waits for them, and re-layouts: 37 us -> 45.7 us
    all_to_all x1, blocking collectives: 98.4 us -> 109 us  [local(): lax.all_to_all(jnp.stack(jnp.split(local_hidden.reshape(tiles, owned, hal...]
    unnamed x15 -> x24, local copies, waits for them, and re-layouts: 6.66 us -> 14.2 us
where the time goes in v1:
time: 375 us; the launch traced here: 368 us
  matrix products  137 us (37%)
  blocking collectives  109 us (29%)
  waiting for transfers between devices  56.1 us (15%)
  local copies, waits for them, and re-layouts  45.7 us (12%)
  between operations  14.7 us (4%)
  starting transfers between devices  5.03 us (1%)
    all_to_all x1, blocking collectives, local(): lax.all_to_all(jnp.stack(jnp.split(local_hidden.reshape(tiles, owned, hal...  109 us
    dot_general x9, matrix products, local(): jnp.dot(window, second_weight[tap_row, tap_col], preferred_element_type=j...  66.8 us
    reduce_scatter x1, waiting for transfers between devices, local(): lax.psum_scatter(jnp.stack(terms, axis=1).reshape(lax.axis_size(('group',...  56.1 us
    dot_general x9, matrix products, local(): lax.dot_general(selected, window, (((0,), (0,)), ((), ())), preferred_ele...  45.4 us
    dot_general x3, matrix products, first_conv(): jnp.dot(sources[tap_row], wide_kernel, preferred_element_type=jnp.float32)  14.9 us
    unnamed x24, local copies, waits for them, and re-layouts  14.2 us
    reshape x1, local copies, waits for them, and re-layouts, first_conv(): paired = source.reshape(images, rows // 2, 2, width // 2, 2 * inputs)  12.9 us
    dot_general x1, matrix products, first_conv(): jnp.dot(shift_cols_right(halves), narrow_kernel, preferred_element_type=j...  10.3 us
  transfers between devices with their start and end apart: 2, of which 1 were waited for; matrix products, arithmetic and copies ran while one was open for 20% of the time, Pallas kernels for 0%

profile of v1, /device:TPU:0, one launch (start us, length us, event | category | flops | bytes accessed | tf_op | source)
XLA Modules:
  0.0 368.3 jit_solution(13994934485233358162)
XLA Ops:
  8.2 5.0 %collective-permute-start = (bf16[8,1,128,128]{3,2,1,0:T(8,128)(2,1)S(1)}, bf16[8,1,128,128]{3,2,1,0:T(8,128)(2,1)S(1)}, u32[]{:S(2)}, u32[]{:S(2)}) collective-permute-start(bf16[8,1,128,128]{3,2,1,0:T(8,128)(2,1)S(1)} %slice.111), channel_id=1, source_target_pairs={{0,1},{1,2},{2,3},{3,4},{4,5},{5,6},{6,7},{8,9},{9,10},{10,11},{11... | collective-permute-start | bytes 786440 | tf_op jit(solution)/shard_map/ppermute | solution.py:10
  13.2 12.9 %reshape.113 = bf16[8,16,2,64,256]{4,3,2,1,0:T(8,128)(2,1)} reshape(bf16[8,32,128,128]{3,2,1,0:T(8,128)(2,1)} %param.4) | data formatting | bytes 16777216 | tf_op jit(solution)/shard_map/reshape | solution.py:26
  26.2 6.8 %fusion.196 = f32[8,16,64,256]{3,2,1,0:T(8,128)} fusion(bf16[256,256,1,1]{1,0,3,2:T(8,128)(2,1)S(1)} %bitcast.286, bf16[8,16,2,64,256]{4,3,2,1,0:T(8,128)(2,1)} %reshape.113), kind=kOutput, calls=%fused_computation.172 | convolution fusion | flops 1073741824 | bytes 12713984 | tf_op jit(solution)/shard_map/dot_general | solution.py:35
  33.1 4.5 %fusion.197 = f32[8,16,64,256]{3,2,1,0:T(8,128)} fusion(bf16[256,256,1,1]{1,0,3,2:T(8,128)(2,1)S(1)} %bitcast.285, bf16[8,16,2,64,256]{4,3,2,1,0:T(8,128)(2,1)S(1)} %bitcast.269), kind=kOutput, calls=%fused_computation.173 | convolution fusion | flops 1073741824 | bytes 12713984 | tf_op jit(solution)/shard_map/dot_general | solution.py:35
  38.7 2.4 slice.143
  41.1 1.8 slice.146
  42.9 1.8 slice.145
  44.8 3.5 fusion.18
  48.4 10.3 %maximum_convert_fusion = bf16[8,16,64,256]{3,2,1,0:T(8,128)(2,1)} fusion(f32[8,16,64,256]{3,2,1,0:T(8,128)} %fusion.196, f32[8,16,64,256]{3,2,1,0:T(8,128)S(1)} %fusion.18, f32[8,16,64,256]{3,2,1,0:T(8,128)} %fusion.197, bf16[384,256,1,1]{1,0,3,2:T(8,128)(2,1)S(1)} %bitcast.283, bf16[8,16,64,128]{3,2,1,0:T(8,128)(2,1)} %slice.146, ...), kind=kOutput, calls=%fused_computation.6 | convolution fusion | flops 1661992960 | bytes 37945344 | tf_op jit(solution)/shard_map/dot_general | solution.py:38
  67.4 109.4 %all_to_all.5 = bf16[8,1,1,16,64,256]{5,4,3,2,1,0:T(8,128)(2,1)S(1)} all-to-all(bf16[8,1,1,16,64,256]{5,4,3,2,1,0:T(8,128)(2,1)S(1)} %fusion.150), channel_id=1, replica_groups=mesh['group'=4,'tile'=8] {'tile'}, dimensions={0} | all-to-all | bytes 8388608 | tf_op jit(solution)/shard_map/all_to_all | solution.py:53
  176.8 2.4 copy.27
  179.3 4.8 %pad_slice_fusion.1 = (bf16[1,130,63,256]{3,1,2,0:T(8,128)(2,1)S(1)}, bf16[1,130,63,256]{3,1,2,0:T(8,128)(2,1)S(1)}) fusion(bf16[1,128,64,256]{3,1,2,0:T(8,128)(2,1)S(1)} %copy.27), kind=kLoop, calls=%fused_computation.79 | loop fusion | bytes 12580864 | tf_op jit(solution)/shard_map/slice | solution.py:15
  184.1 4.5 %fusion.24 = f32[128,64,256]{2,0,1:T(8,128)} fusion(bf16[1,130,63,256]{3,1,2,0:T(8,128)(2,1)S(1)} %get-tuple-element.9, bf16[3,3,256,256]{3,2,1,0:T(8,128)(2,1)S(1)} %copy-done.4), kind=kOutput, calls=%fused_computation.25 | convolution fusion | flops 1073741824 | bytes 12906496 | tf_op jit(solution)/shard_map/dot_general | solution.py:76
  188.6 4.5 %fusion.36 = f32[128,64,256]{2,0,1:T(8,128)} fusion(bf16[1,130,63,256]{3,1,2,0:T(8,128)(2,1)S(1)} %get-tuple-element.9, bf16[3,3,256,256]{3,2,1,0:T(8,128)(2,1)S(1)} %copy-done.4), kind=kOutput, calls=%fused_computation.37 | convolution fusion | flops 1073741824 | bytes 12906496 | tf_op jit(solution)/shard_map/dot_general | solution.py:76
  193.1 4.5 %fusion.32 = f32[128,64,256]{2,0,1:T(8,128)} fusion(bf16[1,130,63,256]{3,1,2,0:T(8,128)(2,1)S(1)} %get-tuple-element.8, bf16[3,3,256,256]{3,2,1,0:T(8,128)(2,1)S(1)} %copy-done.4), kind=kOutput, calls=%fused_computation.33 | convolution fusion | flops 1073741824 | bytes 12906496 | tf_op jit(solution)/shard_map/dot_general | solution.py:76
  197.6 4.5 %fusion.40 = f32[128,64,256]{2,0,1:T(8,128)} fusion(bf16[1,130,63,256]{3,1,2,0:T(8,128)(2,1)S(1)} %get-tuple-element.8, bf16[3,3,256,256]{3,2,1,0:T(8,128)(2,1)S(1)} %copy-done.4), kind=kOutput, calls=%fused_computation.41 | convolution fusion | flops 1073741824 | bytes 12906496 | tf_op jit(solution)/shard_map/dot_general | solution.py:76
  202.1 4.5 %fusion.44 = f32[128,64,256]{2,0,1:T(8,128)} fusion(bf16[1,130,63,256]{3,1,2,0:T(8,128)(2,1)S(1)} %get-tuple-element.9, bf16[3,3,256,256]{3,2,1,0:T(8,128)(2,1)S(1)} %copy-done.4), kind=kOutput, calls=%fused_computation.45 | convolution fusion | flops 1073741824 | bytes 12906496 | tf_op jit(solution)/shard_map/dot_general | solution.py:76
  206.6 4.5 %fusion.52 = f32[128,64,256]{2,0,1:T(8,128)} fusion(bf16[1,130,63,256]{3,1,2,0:T(8,128)(2,1)S(1)} %get-tuple-element.8, bf16[3,3,256,256]{3,2,1,0:T(8,128)(2,1)S(1)} %copy-done.4), kind=kOutput, calls=%fused_computation.53 | convolution fusion | flops 1073741824 | bytes 12906496 | tf_op jit(solution)/shard_map/dot_general | solution.py:76
  211.1 4.5 %fusion.28 = f32[128,64,256]{2,0,1:T(8,128)} fusion(bf16[1,128,64,256]{3,1,2,0:T(8,128)(2,1)S(1)} %copy.27, bf16[3,3,256,256]{3,2,1,0:T(8,128)(2,1)S(1)} %copy-done.4), kind=kOutput, calls=%fused_computation.29 | convolution fusion | flops 1073741824 | bytes 12713984 | tf_op jit(solution)/shard_map/dot_general | solution.py:76
  215.6 5.4 %fusion.96 = f32[256,9,256]{0,2,1:T(8,128)S(1)} fusion(bf16[1,130,63,256]{3,1,2,0:T(8,128)(2,1)S(1)} %get-tuple-element.8, bf16[128,64,256]{2,1,0:T(8,128)(2,1)S(1)} %bitcast.273), kind=kOutput, calls=%fused_computation.93 | convolution fusion | flops 1073741824 | bytes 8649728 | tf_op jit(solution)/shard_map/dot_general | solution.py:87
  221.0 5.6 %fusion.102 = f32[256,9,256]{0,2,1:T(8,128)S(1)} fusion(f32[256,9,256]{0,2,1:T(8,128)S(1)} %fusion.96, bf16[1,128,64,256]{3,1,2,0:T(8,128)(2,1)S(1)} %copy.27, bf16[128,64,256]{2,1,0:T(8,128)(2,1)S(1)} %bitcast.274), kind=kOutput, calls=%fused_computation.95 | convolution fusion | flops 1073741824 | bytes 8650752 | tf_op jit(solution)/shard_map/dot_general | solution.py:87
  226.6 5.2 %fusion.108 = f32[256,9,256]{0,2,1:T(8,128)S(1)} fusion(f32[256,9,256]{0,2,1:T(8,128)S(1)} %fusion.102, bf16[1,130,63,256]{3,1,2,0:T(8,128)(2,1)S(1)} %get-tuple-element.9, bf16[128,64,256]{2,1,0:T(8,128)(2,1)S(1)} %bitcast.275), kind=kOutput, calls=%fused_computation.97 | convolution fusion | flops 1073741824 | bytes 8843264 | tf_op jit(solution)/shard_map/dot_general | solution.py:87
  231.8 5.4 %fusion.114 = f32[256,9,256]{0,2,1:T(8,128)S(1)} fusion(f32[256,9,256]{0,2,1:T(8,128)S(1)} %fusion.108, bf16[1,130,63,256]{3,1,2,0:T(8,128)(2,1)S(1)} %get-tuple-element.8, bf16[128,64,256]{2,1,0:T(8,128)(2,1)S(1)} %bitcast.276), kind=kOutput, calls=%fused_computation.99 | convolution fusion | flops 1073741824 | bytes 8843264 | tf_op jit(solution)/shard_map/dot_general | solution.py:87
  238.6 5.5 %fusion.120 = f32[256,9,256]{0,2,1:T(8,128)S(1)} fusion(f32[256,9,256]{0,2,1:T(8,128)S(1)} %fusion.141, bf16[1,130,63,256]{3,1,2,0:T(8,128)(2,1)S(1)} %get-tuple-element.9, bf16[128,64,256]{2,1,0:T(8,128)(2,1)S(1)} %bitcast.278), kind=kOutput, calls=%fused_computation.101 | convolution fusion | flops 1073741824 | bytes 8843264 | tf_op jit(solution)/shard_map/dot_general | solution.py:87
  244.2 5.5 %fusion.126 = f32[256,9,256]{0,2,1:T(8,128)S(1)} fusion(f32[256,9,256]{0,2,1:T(8,128)S(1)} %fusion.120, bf16[1,130,63,256]{3,1,2,0:T(8,128)(2,1)S(1)} %get-tuple-element.8, bf16[128,64,256]{2,1,0:T(8,128)(2,1)S(1)} %bitcast.279), kind=kOutput, calls=%fused_computation.103 | convolution fusion | flops 1073741824 | bytes 8843264 | tf_op jit(solution)/shard_map/dot_general | solution.py:87
  249.6 5.6 %fusion.132 = f32[256,9,256]{0,2,1:T(8,128)S(1)} fusion(f32[256,9,256]{0,2,1:T(8,128)S(1)} %fusion.126, bf16[1,128,64,256]{3,1,2,0:T(8,128)(2,1)S(1)} %copy.27, bf16[128,64,256]{2,1,0:T(8,128)(2,1)S(1)} %bitcast.280), kind=kOutput, calls=%fused_computation.105 | convolution fusion | flops 1073741824 | bytes 8650752 | tf_op jit(solution)/shard_map/dot_general | solution.py:87
  255.3 5.8 %fusion.138 = f32[256,9,256]{0,2,1:T(8,128)S(1)} fusion(f32[256,9,256]{0,2,1:T(8,128)S(1)} %fusion.132, bf16[1,130,63,256]{3,1,2,0:T(8,128)(2,1)S(1)} %get-tuple-element.9, bf16[128,64,256]{2,1,0:T(8,128)(2,1)S(1)} %bitcast.281), kind=kOutput, calls=%fused_computation.107 | convolution fusion | flops 1073741824 | bytes 8843264 | tf_op jit(solution)/shard_map/dot_general | solution.py:87
  261.0 2.0 copy.45
  263.0 6.7 %fusion.48 = f32[128,64,256]{2,0,1:T(8,128)} fusion(bf16[1,128,64,256]{3,1,2,0:T(8,128)(2,1)} %copy-done.1, bf16[3,3,256,256]{3,2,1,0:T(8,128)(2,1)S(1)} %copy-done.4), kind=kOutput, calls=%fused_computation.49 | convolution fusion | flops 1073741824 | bytes 12713984 | tf_op jit(solution)/shard_map/dot_general | solution.py:76
  269.7 28.6 %fusion.17 = bf16[1,128,64,256]{3,1,2,0:T(8,128)(2,1)} fusion(f32[128,64,256]{2,0,1:T(8,128)} %fusion.24, f32[128,64,256]{2,0,1:T(8,128)} %fusion.28, f32[128,64,256]{2,0,1:T(8,128)} %fusion.32, f32[128,64,256]{2,0,1:T(8,128)} %fusion.36, f32[128,64,256]{2,0,1:T(8,128)} %fusion.40, f32[128,64,256]{2,0,1:T(8,128)} %fusion.44, f32[128,64,256]{2,0,1:T(8,128)} %fusion.52, ...), kind=kOutput, calls=%fused_computation.16 | convolution fusion | flops 1092616192 | bytes 75628544 | tf_op jit(solution)/shard_map/dot_general | solution.py:76
  298.3 6.6 %copy.46 = bf16[1,128,64,256]{3,2,1,0:T(8,128)(2,1)} copy(bf16[1,128,64,256]{3,1,2,0:T(8,128)(2,1)} %fusion.17) | data formatting | bytes 8388608
  304.9 56.1 %reduce-scatter.2.cloned.1.call-done = f32[8,2304]{1,0:T(8,128)} async-done(((f32[256,2304]{1,0:T(8,128)}), f32[8,2304]{1,0:T(8,128)}) %reduce-scatter.2.cloned.1.call-update) | async-done | bytes 73744 | tf_op jit(solution)/shard_map/reduce_scatter | solution.py:91
  (35 shorter events, 12.4 us)
Async XLA Ops:
  7.2 353.9 %reduce-scatter.2.cloned.1.call-start = ((), (), s32[]{:S(2)}) async-start(), calls=%async_computation.2 | async-start | bytes 2433024 | tf_op jit(solution)/shard_map/reduce_scatter | solution.py:91
  8.2 18.0 %copy-start.5 = (bf16[3,3,128,256]{3,2,1,0:T(8,128)(2,1)S(1)}, bf16[3,3,128,256]{3,2,1,0:T(8,128)(2,1)}, u32[]{:S(2)}) copy-start(bf16[3,3,128,256]{3,2,1,0:T(8,128)(2,1)} %param.5) | copy-start | bytes 1769476
  8.2 36.5 %collective-permute-start = (bf16[8,1,128,128]{3,2,1,0:T(8,128)(2,1)S(1)}, bf16[8,1,128,128]{3,2,1,0:T(8,128)(2,1)S(1)}, u32[]{:S(2)}, u32[]{:S(2)}) collective-permute-start(bf16[8,1,128,128]{3,2,1,0:T(8,128)(2,1)S(1)} %slice.111), channel_id=1, source_target_pairs={{0,1},{1,2},{2,3},{3,4},{4,5},{5,6},{6,7},{8,9},{9,10},{10,11},{11... | collective-permute-start | bytes 786440 | tf_op jit(solution)/shard_map/ppermute | solution.py:10
  26.2 6.9 %slice-start = ((s8[8388608]{0:T(1024)(128)(4,1)}), s8[4194304]{0:T(1024)(128)(4,1)S(1)}, s32[]{:S(2)}) async-start(s8[8388608]{0:T(1024)(128)(4,1)} %bitcast.268), calls=%async_computation.3 | async-start | bytes 8388608
  26.2 6.9 %slice-start.1 = ((s8[8388608]{0:T(1024)(128)(4,1)}), s8[4194304]{0:T(1024)(128)(4,1)S(1)}, s32[]{:S(2)}) async-start(s8[8388608]{0:T(1024)(128)(4,1)} %bitcast.268), calls=%async_computation.4 | async-start | bytes 8388608
  44.8 3.5 copy-start.2
  44.8 3.5 slice-start.2
  176.8 60.4 %copy-start = (bf16[8,1,1,16,64,256]{5,4,3,2,1,0:T(8,128)(2,1)}, bf16[8,1,1,16,64,256]{5,4,3,2,1,0:T(8,128)(2,1)S(1)}, u32[]{:S(2)}) copy-start(bf16[8,1,1,16,64,256]{5,4,3,2,1,0:T(8,128)(2,1)S(1)} %all_to_all.5) | copy-start | bytes 12582916
  179.2 70.4 %copy-start.1 = (bf16[1,128,64,256]{3,1,2,0:T(8,128)(2,1)}, bf16[1,128,64,256]{3,1,2,0:T(8,128)(2,1)S(1)}, u32[]{:S(2)}) copy-start(bf16[1,128,64,256]{3,1,2,0:T(8,128)(2,1)S(1)} %copy.27) | copy-start | bytes 12582916
  179.3 4.8 %copy-start.4 = (bf16[3,3,256,256]{3,2,1,0:T(8,128)(2,1)S(1)}, bf16[3,3,256,256]{3,2,1,0:T(8,128)(2,1)}, u32[]{:S(2)}) copy-start(bf16[3,3,256,256]{3,2,1,0:T(8,128)(2,1)} %param.6) | copy-start | bytes 3538948
  211.1 4.5 %copy-start.3 = (bf16[1,128,64,256]{3,2,1,0:T(8,128)(2,1)S(1)}, bf16[1,128,64,256]{3,2,1,0:T(8,128)(2,1)}, u32[]{:S(2)}) copy-start(bf16[1,128,64,256]{3,2,1,0:T(8,128)(2,1)} %param.7) | copy-start | bytes 12582916
Sparse Core Ops, SparseCore 0:
  263.1 97.8 reduce-scatter.1
